TPU v7x, 256 devices: a whole 4x4x8 slice. The times are simulated.
256 devices in a mesh: req: 64 (over z, x, core), tp: 4 (over y).
Axes of the slice: x: 4, y: 4, z: 8, core: 2. Of those that a mesh axis runs over, the one named last changes fastest.
Arguments:
- hidden: bfloat16 [16384, 2048], P('req'), may hold values from -10.5 to 10.5
- lengths: int32 [64], replicated, may hold values from 1 to 1024, 16384 in all
- dealing: int32 [64], replicated, may hold values from 0 to 63, each once
- norm_gain: bfloat16 [2048], replicated, may hold values from 0.5 to 1.5
- w_query: bfloat16 [2048, 2048], P(None, 'tp'), may hold values from -0.125 to 0.125
- w_key: bfloat16 [2048, 1024], P(None, 'tp'), may hold values from -0.125 to 0.125
- w_value: bfloat16 [2048, 1024], P(None, 'tp'), may hold values from -0.125 to 0.125
- query_gain: bfloat16 [128], replicated, may hold values from 0.5 to 8
- key_gain: bfloat16 [128], replicated, may hold values from 0.5 to 8
- w_out: bfloat16 [2048, 2048], P(None, 'tp'), may hold values from -0.125 to 0.125
Outputs:
- hidden_out: bfloat16 [16384, 2048], P('req', 'tp')
- kv_cache: bfloat16 [2, 64, 1024, 1024], P(None, 'req', None, 'tp')
Inputs may be any that keep to these rules, and one draw needn't show every extreme that they name: The lengths sum to 16384; the largest is exactly 1024. A permutation: dealt slot j, on device j of req, holds prompt dealing[j].
All inputs are finite; a program needn't handle non-finite values.
Results may differ from a plain program's by a relative error of at most 0.012.
The roundings to bfloat16 on the way count: a program that leaves them out, or rounds other values in their place, can miss the bound.
Values may be sent and summed in bfloat16 or wider, within the bound.
No kernel may reach another device: no remote copies, remote signals or barrier semaphores. Data moves between devices by JAX's collectives and lax.ppermute only.
A program may use at most 128 MiB of HBM per device.

v0:
```python
import jax
import jax.numpy as jnp
from jax import lax
from jax.sharding import PartitionSpec as P

EPS = 1e-06
THETA = 1000000.0


def rms_rows(values, scale_gain):
    inv_rms = lax.rsqrt(jnp.mean(values * values, axis=-1, keepdims=True) + EPS)
    return values * inv_rms * scale_gain


def rotate(values, positions):
    features = values.shape[-1]
    half_width = features // 2
    frequency = THETA ** (-(jnp.arange(half_width).astype(jnp.float32) * 2.0) / features)
    angles = positions.astype(jnp.float32)[:, None] * frequency[None, :]
    cosine = jnp.cos(angles)[:, None, :]
    sine_part = jnp.sin(angles)[:, None, :]
    first_half = values[..., :half_width]
    second_half = values[..., half_width:]
    return jnp.concatenate(
        [
            first_half * cosine - second_half * sine_part,
            second_half * cosine + first_half * sine_part,
        ],
        axis=-1,
    )


def project(normed, w_query, w_key, w_value, query_gain, key_gain, positions):
    head_dim = query_gain.shape[0]
    row_count = normed.shape[0]
    query_rows = jnp.dot(normed, w_query, preferred_element_type=jnp.float32).reshape(
        row_count, -1, head_dim
    )
    key_rows = jnp.dot(normed, w_key, preferred_element_type=jnp.float32).reshape(
        row_count, -1, head_dim
    )
    value_rows = jnp.dot(normed, w_value, preferred_element_type=jnp.float32).astype(jnp.bfloat16)
    query_rows = rotate(rms_rows(query_rows, query_gain.astype(jnp.float32)), positions).astype(
        jnp.bfloat16
    )
    key_rows = rotate(rms_rows(key_rows, key_gain.astype(jnp.float32)), positions).astype(
        jnp.bfloat16
    )
    return (query_rows.reshape(row_count, -1), key_rows.reshape(row_count, -1), value_rows)


def attend(query_slot, key_slot, value_slot, prompt_length, head_dim):
    slot_len, query_width = query_slot.shape
    kv_heads = key_slot.shape[1] // head_dim
    group_size = query_width // head_dim // kv_heads
    queries = query_slot.reshape(slot_len, kv_heads, group_size, head_dim)
    keys_split = key_slot.reshape(slot_len, kv_heads, head_dim)
    values_split = value_slot.reshape(slot_len, kv_heads, head_dim)
    scores = jnp.einsum(
        "qkgd,skd->kgqs", queries, keys_split, preferred_element_type=jnp.float32
    ) * head_dim ** (-0.5)
    offsets = jnp.arange(slot_len, dtype=jnp.int32)
    allowed = (offsets[None, :] <= offsets[:, None]) & (offsets[None, :] < prompt_length)
    scores = jnp.where(allowed[None, None], scores, -jnp.inf)
    row_max = jnp.max(scores, axis=-1, keepdims=True)
    weights = jnp.exp(scores - row_max)
    weights = (weights / jnp.sum(weights, axis=-1, keepdims=True)).astype(jnp.bfloat16)
    mixture = jnp.einsum(
        "kgqs,skd->qkgd", weights, values_split, preferred_element_type=jnp.float32
    )
    return mixture.astype(jnp.bfloat16).reshape(slot_len, query_width)


def on_device(
    hidden, lengths, dealing, norm_gain, w_query, w_key, w_value, query_gain, key_gain, w_out
):
    devices = lax.axis_size("req")
    home_index = lax.axis_index("req")
    slice_index = lax.axis_index("tp")
    tok_rows, features = hidden.shape
    head_dim = query_gain.shape[0]
    out_width = w_out.shape[1]
    slot_len = 4 * tok_rows
    capacity = slot_len // devices
    prompt_total = lengths.shape[0]
    prompt_ids = jnp.arange(prompt_total, dtype=jnp.int32)
    prompt_ends = jnp.cumsum(lengths)
    starts = prompt_ends - lengths
    packed_ids = jnp.arange(tok_rows, dtype=jnp.int32) * devices + home_index
    segment = jnp.sum((packed_ids[:, None] >= prompt_ends[None, :]).astype(jnp.int32), axis=1)
    seg_onehot = (segment[:, None] == prompt_ids[None, :]).astype(jnp.int32)
    positions = packed_ids - jnp.sum(seg_onehot * starts[None, :], axis=1)
    inverse = jnp.zeros((prompt_total,), jnp.int32).at[dealing].set(prompt_ids)
    deal_hot = (dealing[:, None] == prompt_ids[None, :]).astype(jnp.int32)
    dealt_starts = jnp.sum(deal_hot * starts[None, :], axis=1)
    dealt_lengths = jnp.sum(deal_hot * lengths[None, :], axis=1)
    first_offset = jnp.mod(home_index - dealt_starts, devices)
    ranks = jnp.arange(capacity, dtype=jnp.int32)
    slot_offset = first_offset[None, :] + ranks[:, None] * devices
    send_valid = slot_offset < dealt_lengths[None, :]
    send_rows = jnp.where(
        send_valid, (dealt_starts[None, :] + slot_offset - home_index) // devices, 0
    ).reshape(-1)
    my_start = lax.dynamic_index_in_dim(dealt_starts, home_index, 0, keepdims=False)
    my_length = lax.dynamic_index_in_dim(dealt_lengths, home_index, 0, keepdims=False)
    roll_shift = jnp.mod(my_start, devices)
    my_slots = jnp.sum(seg_onehot * inverse[None, :], axis=1)
    back_rows = positions // devices * devices + my_slots
    offsets = jnp.arange(slot_len, dtype=jnp.int32)
    gain_values = norm_gain.astype(jnp.float32)
    picked = jnp.take(hidden, send_rows, axis=0).reshape(capacity, devices, hidden.shape[1])
    arrived = lax.all_to_all(
        jnp.where(send_valid[:, :, None], picked, jnp.zeros((), hidden.dtype)),
        "req",
        split_axis=1,
        concat_axis=1,
        tiled=True,
    )
    slot_hidden = jnp.roll(arrived, -roll_shift, axis=1).reshape(slot_len, arrived.shape[2])
    normed = rms_rows(slot_hidden.astype(jnp.float32), gain_values).astype(jnp.bfloat16)
    query_slot, key_slot, value_slot = project(
        normed, w_query, w_key, w_value, query_gain, key_gain, offsets
    )
    mixture = attend(query_slot, key_slot, value_slot, my_length, head_dim)
    sendback = jnp.roll(mixture.reshape(capacity, devices, mixture.shape[1]), roll_shift, axis=1)
    returned = lax.all_to_all(sendback, "req", split_axis=1, concat_axis=1, tiled=True)
    attended = jnp.take(returned.reshape(capacity * devices, -1), back_rows, axis=0)
    kv_cache = jnp.stack([key_slot, value_slot])[:, None]
    summed = jnp.dot(
        lax.all_gather(attended, "tp", axis=1, tiled=True),
        w_out,
        preferred_element_type=jnp.float32,
    )
    branch = lax.optimization_barrier(summed.astype(jnp.bfloat16))
    residual = lax.dynamic_slice_in_dim(hidden, slice_index * out_width, out_width, 1)
    hidden_out = (residual.astype(jnp.float32) + branch.astype(jnp.float32)).astype(jnp.bfloat16)
    return (hidden_out, kv_cache)


def solution(mesh):
    in_specs = (
        P("req", None),
        P(),
        P(),
        P(),
        P(None, "tp"),
        P(None, "tp"),
        P(None, "tp"),
        P(),
        P(),
        P(None, "tp"),
    )
    out_specs = (P("req", "tp"), P(None, "req", None, "tp"))
    return jax.shard_map(
        on_device, mesh=mesh, in_specs=in_specs, out_specs=out_specs, check_vma=False
    )
```

profile of v0, /device:TPU:2, one launch (start us, length us, event | category | flops | bytes accessed | tf_op | source)
XLA Modules:
  0.0 272.4 jit_solution(343829114084428690)
XLA Ops:
  11.1 10.2 %gather_fusion = bf16[1024,2048]{1,0:T(8,128)(2,1)} fusion(bf16[256,2048]{1,0:T(8,128)(2,1)} %param.10, s32[1024]{0:T(1024)S(1)} %broadcast_clamp_fusion), kind=kCustom, calls=%fused_computation | custom fusion | bytes 8392704 | tf_op jit(solution)/shard_map/jit(_take)/gather | solution.py:111
  21.3 9.6 %fusion.10 = bf16[16,64,2048]{2,0,1:T(8,128)(2,1)} fusion(bf16[16,64,2048]{2,1,0:T(8,128)(2,1)} %bitcast.70, pred[16,64]{0,1:T(8,128)(4,1)S(1)} %copy.60, pred[16,64]{0,1:T(8,128)(4,1)S(1)} %copy.59), kind=kLoop, calls=%fused_computation.22 | loop fusion | flops 4194304 | bytes 8390656 | tf_op jit(solution)/shard_map/jit(_where)/select_n | solution.py:113
  30.9 12.3 %all-to-all-start = ((bf16[16,64,2048]{2,0,1:T(8,128)(2,1)}), bf16[16,64,2048]{2,0,1:T(8,128)(2,1)}, u32[]{:S(2)}, u32[]{:S(2)}) async-start(bf16[16,64,2048]{2,0,1:T(8,128)(2,1)} %fusion.10), calls=%async_computation | async-start | bytes 8388608 | tf_op jit(solution)/shard_map/all_to_all | solution.py:112
  46.4 4.0 %copy.80 = bf16[512,2048]{1,0:T(8,128)(2,1)} copy(bf16[512,2048]{0,1:T(8,128)(2,1)} %bitcast.76) | data formatting | bytes 4194304 | tf_op jit(solution)/shard_map/dot_general | solution.py:36
  54.9 84.4 %all-to-all-done = bf16[16,64,2048]{2,0,1:T(8,128)(2,1)} async-done(((bf16[16,64,2048]{2,0,1:T(8,128)(2,1)}), bf16[16,64,2048]{2,0,1:T(8,128)(2,1)}, u32[]{:S(2)}, u32[]{:S(2)}) %all-to-all-start) | async-done | bytes 4194336 | tf_op jit(solution)/shard_map/all_to_all | solution.py:112
  139.3 4.5 %copy.62 = bf16[16,64,2048]{2,1,0:T(8,128)(2,1)S(1)} copy(bf16[16,64,2048]{2,0,1:T(8,128)(2,1)} %all-to-all-done) | data formatting | bytes 8388608 | tf_op jit(solution)/shard_map/all_to_all | solution.py:112
  143.8 6.5 %multiply_reduce_fusion = (f32[16,64]{1,0:T(8,128)S(1)}, f32[16,64,2048]{2,1,0:T(8,128)}) fusion(s32[]{:T(128)S(6)} %select_n.166, bf16[16,64,2048]{2,1,0:T(8,128)(2,1)S(1)} %copy.62), kind=kLoop, calls=%fused_computation.16 | loop fusion | flops 12581888 | bytes 12587012 | tf_op jit(solution)/shard_map/reduce_sum | solution.py:11
  150.3 4.3 %multiply_convert_fusion = bf16[16,64,2048]{2,1,0:T(8,128)(2,1)S(1)} fusion(f32[16,64,2048]{2,1,0:T(8,128)} %get-tuple-element.17, f32[2048]{0:T(1024)S(1)} %convert_element_type.122, f32[16,64]{1,0:T(8,128)S(1)} %add_rsqrt_fusion.2), kind=kLoop, calls=%fused_computation.15 | loop fusion | flops 6291456 | bytes 12595200 | tf_op jit(solution)/shard_map/convert_element_type | solution.py:120
  154.6 1.5 copy-done.1
  156.1 2.7 fusion.3
  159.5 2.4 multiply_reduce_fusion.1
  163.6 2.4 copy.67
  167.4 3.9 %multiply_reduce_fusion.2 = (f32[1024,2]{0,1:T(2,128)S(1)}, f32[1024,2,128]{0,2,1:T(8,128)S(1)}) fusion(bf16[1024,2048,1]{1,0,2:T(8,128)(2,1)} %bitcast.73, bf16[2,128,2048]{2,1,0:T(8,128)(2,1)} %bitcast.80), kind=kOutput, calls=%fused_computation.41 | convolution fusion | flops 1074264064 | bytes 6299648 | tf_op jit(solution)/shard_map/dot_general | solution.py:39
  173.6 2.1 convolution_convert_fusion
  175.7 11.5 %fusion.38 = (f32[2,2,1024]{2,1,0:T(2,128)S(1)}, f32[2,2,1024,1024]{2,3,1,0:T(8,128)}) fusion(pred[1024,1024]{0,1:T(8,128)(4,1)S(1)} %copy-done.5, bf16[1024,2,2,64]{3,0,2,1:T(8,128)(2,1)} %copy.67, bf16[1024,2,2,64]{3,0,2,1:T(8,128)(2,1)} %copy.66, bf16[1024,2,64]{0,2,1:T(8,128)(2,1)} %get-tuple-element.21, bf16[1024,2,64]{0,2,1:T(8,128)(2,1)S(1)} %get-tuple-element.20), kind=kOutput, calls=%fused_computation.108 | convolution fusion | flops 1093665792 | bytes 19415040 | tf_op jit(solution)/shard_map/sub | solution.py:66
  187.1 7.2 %fusion.15 = bf16[1024,2,2,128]{0,3,2,1:T(8,128)(2,1)S(1)} fusion(bf16[1024,2,128,1]{0,2,3,1:T(8,128)(2,1)} %bitcast.81, f32[2,2,1024,1024]{2,3,1,0:T(8,128)} %get-tuple-element.31, f32[2,2,1024]{2,1,0:T(2,128)S(1)} %get-tuple-element.30), kind=kOutput, calls=%fused_computation.31 | convolution fusion | flops 1082654720 | bytes 18366464 | tf_op jit(solution)/shard_map/kgqs,skd->qkgd/dot_general | solution.py:68
  194.4 2.0 copy.70
  198.7 1.5 copy.71
  200.3 5.6 %all-to-all-start.1 = ((bf16[16,64,512]{2,0,1:T(8,128)(2,1)}), bf16[16,64,512]{2,0,1:T(8,128)(2,1)}, u32[]{:S(2)}, u32[]{:S(2)}) async-start(bf16[16,64,512]{2,0,1:T(8,128)(2,1)} %copy.71), calls=%async_computation.1 | async-start | bytes 2097152 | tf_op jit(solution)/shard_map/all_to_all | solution.py:126
  207.0 27.6 %all-to-all-done.1 = bf16[16,64,512]{2,0,1:T(8,128)(2,1)} async-done(((bf16[16,64,512]{2,0,1:T(8,128)(2,1)}), bf16[16,64,512]{2,0,1:T(8,128)(2,1)}, u32[]{:S(2)}, u32[]{:S(2)}) %all-to-all-start.1) | async-done | bytes 1048608 | tf_op jit(solution)/shard_map/all_to_all | solution.py:126
  234.6 1.8 copy.72
  242.0 20.0 %all-gather.2.cloned.1.call-done = bf16[256,2048]{1,0:T(8,128)(2,1)} async-done(((bf16[256,512]{1,0:T(8,128)(2,1)}), bf16[256,2048]{1,0:T(8,128)(2,1)}) %all-gather.2.cloned.1.call-update) | async-done | bytes 1048592 | tf_op jit(solution)/shard_map/all_gather | solution.py:130
  261.9 1.9 convolution_convert_fusion.1
  263.9 1.7 add_convert_fusion.1
  (75 shorter events, 24.5 us)
Async XLA Ops:
  7.2 254.8 %copy-start = (bf16[2048,512]{1,0:T(8,128)(2,1)S(1)}, bf16[2048,512]{1,0:T(8,128)(2,1)}, u32[]{:S(2)}) copy-start(bf16[2048,512]{1,0:T(8,128)(2,1)} %param.19) | copy-start | bytes 6291460
  30.9 15.6 %copy-start.8 = (bf16[2048]{0:T(1024)(128)(2,1)S(1)}, bf16[2048]{0:T(1024)(128)(2,1)}, u32[]{:S(2)}) copy-start(bf16[2048]{0:T(1024)(128)(2,1)} %param.13) | copy-start | bytes 12292
  30.9 108.4 %all-to-all-start = ((bf16[16,64,2048]{2,0,1:T(8,128)(2,1)}), bf16[16,64,2048]{2,0,1:T(8,128)(2,1)}, u32[]{:S(2)}, u32[]{:S(2)}) async-start(bf16[16,64,2048]{2,0,1:T(8,128)(2,1)} %fusion.10), calls=%async_computation | async-start | bytes 8388608 | tf_op jit(solution)/shard_map/all_to_all | solution.py:112
  43.2 7.2 %copy-start.10 = (bf16[128]{0:T(256)(128)(2,1)S(1)}, bf16[128]{0:T(256)(128)(2,1)}, u32[]{:S(2)}) copy-start(bf16[128]{0:T(256)(128)(2,1)} %param.17) | copy-start | bytes 772
  43.2 7.2 %copy-start.6 = (bf16[2048,256]{1,0:T(8,128)(2,1)S(1)}, bf16[2048,256]{1,0:T(8,128)(2,1)}, u32[]{:S(2)}) copy-start(bf16[2048,256]{1,0:T(8,128)(2,1)} %param.15) | copy-start | bytes 3145732
  43.2 8.6 %copy-start.11 = (bf16[128]{0:T(256)(128)(2,1)S(1)}, bf16[128]{0:T(256)(128)(2,1)}, u32[]{:S(2)}) copy-start(bf16[128]{0:T(256)(128)(2,1)} %param.18) | copy-start | bytes 772
  150.3 5.8 %copy-start.1 = (f32[16,64,2048]{2,1,0:T(8,128)S(1)}, f32[16,64,2048]{2,1,0:T(8,128)}, u32[]{:S(2)}) copy-start(f32[16,64,2048]{2,1,0:T(8,128)} %get-tuple-element.17) | copy-start | bytes 25165828
  156.1 3.4 %copy-start.3 = (bf16[16,64,2048]{2,1,0:T(8,128)(2,1)}, bf16[16,64,2048]{2,1,0:T(8,128)(2,1)S(1)}, u32[]{:S(2)}) copy-start(bf16[16,64,2048]{2,1,0:T(8,128)(2,1)S(1)} %multiply_convert_fusion) | copy-start | bytes 12582916
  156.1 3.4 %copy-start.4 = (bf16[512,2048]{1,0:T(8,128)(2,1)S(1)}, bf16[512,2048]{1,0:T(8,128)(2,1)}, u32[]{:S(2)}) copy-start(bf16[512,2048]{1,0:T(8,128)(2,1)} %copy.80) | copy-start | bytes 6291460
  167.4 5.0 %copy-start.9 = (bf16[2048,256]{1,0:T(8,128)(2,1)S(1)}, bf16[2048,256]{1,0:T(8,128)(2,1)}, u32[]{:S(2)}) copy-start(bf16[2048,256]{1,0:T(8,128)(2,1)} %param.16) | copy-start | bytes 3145732
  171.3 2.3 copy-start.2
  173.6 2.1 copy-start.7
  173.6 2.1 copy-start.5
  200.3 34.4 %all-to-all-start.1 = ((bf16[16,64,512]{2,0,1:T(8,128)(2,1)}), bf16[16,64,512]{2,0,1:T(8,128)(2,1)}, u32[]{:S(2)}, u32[]{:S(2)}) async-start(bf16[16,64,512]{2,0,1:T(8,128)(2,1)} %copy.71), calls=%async_computation.1 | async-start | bytes 2097152 | tf_op jit(solution)/shard_map/all_to_all | solution.py:126
  205.9 56.0 %all-gather.2.cloned.1.call-start = ((), (), s32[]{:S(2)}) async-start(), calls=%async_computation.2 | async-start | bytes 1310720 | tf_op jit(solution)/shard_map/all_gather | solution.py:130
Sparse Core Ops, SparseCore 0:
  238.6 23.3 all-gather.1
where the time goes:
time: 273 us; the launch traced here: 272 us
  waiting for transfers between devices  132 us (48%)
  local copies, waits for them, and re-layouts  39.9 us (15%)
  other arithmetic  37.2 us (14%)
  matrix products  29 us (11%)
  starting transfers between devices  18 us (7%)
  between operations  16.3 us (6%)
    all_to_all x1, waiting for transfers between devices, on_device(): lax.all_to_all(jnp.where(send_valid[:, :, None], picked, jnp.zeros((), hi...  84.4 us
    all_to_all x1, waiting for transfers between devices, on_device(): lax.all_to_all(sendback, 'req', split_axis=1, concat_axis=1, tiled=True)  27.6 us
    all_gather x1, waiting for transfers between devices, on_device(): lax.all_gather(attended, 'tp', axis=1, tiled=True)  20 us
    all_to_all x1, starting transfers between devices, on_device(): lax.all_to_all(jnp.where(send_valid[:, :, None], picked, jnp.zeros((), hi...  12.3 us
    sub x1, matrix products, attend(): weights = jnp.exp(scores - row_max)  11.5 us
    gather x1, local copies, waits for them, and re-layouts, on_device(): jnp.take(hidden, send_rows, axis=0)  10.2 us
    select_n x1, other arithmetic, on_device(): jnp.where(send_valid[:, :, None], picked, jnp.zeros((), hidden.dtype))  9.61 us
    dot_general x1, matrix products, attend(): jnp.einsum('kgqs,skd->qkgd', weights, values_split, preferred_element_typ...  7.24 us
  transfers between devices with their start and end apart: 3, of which 3 were waited for; matrix products, arithmetic and copies ran while one was open for 5% of the time, Pallas kernels for 0%

commit v1 on v0

--- a/solution.py
+++ b/solution.py
@@ -1,3 +1,4 @@
+import functools
 import jax
 import jax.numpy as jnp
 from jax import lax
@@ -5,6 +6,15 @@
 
 EPS = 1e-06
 THETA = 1000000.0
+
+
+def try_all_roots(m, net_axis):
+    w1 = jnp.stack([m for _ in range(lax.axis_size(net_axis))], 0)
+    opened = lax.all_to_all(w1, split_axis=0, axis_name=net_axis, concat_axis=0)
+    return jnp.concatenate(opened, axis=1)
+
+
+plate_make = functools.partial(try_all_roots, net_axis="tp")
 
 
 def rms_rows(values, scale_gain):
@@ -126,11 +136,7 @@
     returned = lax.all_to_all(sendback, "req", split_axis=1, concat_axis=1, tiled=True)
     attended = jnp.take(returned.reshape(capacity * devices, -1), back_rows, axis=0)
     kv_cache = jnp.stack([key_slot, value_slot])[:, None]
-    summed = jnp.dot(
-        lax.all_gather(attended, "tp", axis=1, tiled=True),
-        w_out,
-        preferred_element_type=jnp.float32,
-    )
+    summed = jnp.dot(plate_make(attended), w_out, preferred_element_type=jnp.float32)
     branch = lax.optimization_barrier(summed.astype(jnp.bfloat16))
     residual = lax.dynamic_slice_in_dim(hidden, slice_index * out_width, out_width, 1)
     hidden_out = (residual.astype(jnp.float32) + branch.astype(jnp.float32)).astype(jnp.bfloat16)

time: 273 us -> 256 us (0.938)
  between operations: 16.3 us -> 2.92 us
  waiting for transfers between devices: 132 us -> 124 us
  starting transfers between devices: 18 us -> 22.4 us
    all_gather x1 -> x0, waiting for transfers between devices: 20 us -> none  [on_device(): lax.all_gather(attended, 'tp', axis=1, tiled=True)]
    all_to_all x0 -> x1, waiting for transfers between devices: none -> 11.8 us  [try_all_roots(): opened = lax.all_to_all(w1, split_axis=0, axis_name=net_axis, concat_axis=0)]
    all_to_all x0 -> x1, starting transfers between devices: none -> 4.46 us  [try_all_roots(): opened = lax.all_to_all(w1, split_axis=0, axis_name=net_axis, concat_axis=0)]
where the time goes in v1:
time: 256 us; the launch traced here: 255 us
  waiting for transfers between devices  124 us (48%)
  local copies, waits for them, and re-layouts  41.1 us (16%)
  other arithmetic  35.5 us (14%)
  matrix products  29 us (11%)
  starting transfers between devices  22.4 us (9%)
  between operations  2.92 us (1%)
    all_to_all x1, waiting for transfers between devices, on_device(): lax.all_to_all(jnp.where(send_valid[:, :, None], picked, jnp.zeros((), hi...  84.4 us
    all_to_all x1, waiting for transfers between devices, on_device(): lax.all_to_all(sendback, 'req', split_axis=1, concat_axis=1, tiled=True)  27.7 us
    all_to_all x1, starting transfers between devices, on_device(): lax.all_to_all(jnp.where(send_valid[:, :, None], picked, jnp.zeros((), hi...  12.3 us
    all_to_all x1, waiting for transfers between devices, try_all_roots(): opened = lax.all_to_all(w1, split_axis=0, axis_name=net_axis, concat_axis=0)  11.8 us
    sub x1, matrix products, attend(): weights = jnp.exp(scores - row_max)  11.5 us
    gather x1, local copies, waits for them, and re-layouts, on_device(): jnp.take(hidden, send_rows, axis=0)  10.2 us
    select_n x1, other arithmetic, on_device(): jnp.where(send_valid[:, :, None], picked, jnp.zeros((), hidden.dtype))  9.61 us
    dot_general x1, matrix products, attend(): jnp.einsum('kgqs,skd->qkgd', weights, values_split, preferred_element_typ...  7.24 us
  transfers between devices with their start and end apart: 3, of which 3 were waited for; matrix products, arithmetic and copies ran while one was open for 5% of the time, Pallas kernels for 0%

profile of v1, /device:TPU:2, one launch (start us, length us, event | category | flops | bytes accessed | tf_op | source)
XLA Modules:
  0.0 254.9 jit_solution(9027542502763500314)
XLA Ops:
  4.5 10.2 %gather_fusion = bf16[1024,2048]{1,0:T(8,128)(2,1)} fusion(bf16[256,2048]{1,0:T(8,128)(2,1)} %param.10, s32[1024]{0:T(1024)S(1)} %broadcast_clamp_fusion), kind=kCustom, calls=%fused_computation | custom fusion | bytes 8392704 | tf_op jit(solution)/shard_map/jit(_take)/gather | solution.py:121
  14.7 9.6 %fusion.10 = bf16[16,64,2048]{2,0,1:T(8,128)(2,1)} fusion(bf16[16,64,2048]{2,1,0:T(8,128)(2,1)} %bitcast.73, pred[16,64]{0,1:T(8,128)(4,1)S(1)} %copy.63, pred[16,64]{0,1:T(8,128)(4,1)S(1)} %copy.62), kind=kLoop, calls=%fused_computation.22 | loop fusion | flops 4194304 | bytes 8390656 | tf_op jit(solution)/shard_map/jit(_where)/select_n | solution.py:123
  24.3 12.3 %all-to-all-start = ((bf16[16,64,2048]{2,0,1:T(8,128)(2,1)}), bf16[16,64,2048]{2,0,1:T(8,128)(2,1)}, u32[]{:S(2)}, u32[]{:S(2)}) async-start(bf16[16,64,2048]{2,0,1:T(8,128)(2,1)} %fusion.10), calls=%async_computation | async-start | bytes 8388608 | tf_op jit(solution)/shard_map/all_to_all | solution.py:122
  39.9 4.0 %copy.84 = bf16[512,2048]{1,0:T(8,128)(2,1)} copy(bf16[512,2048]{0,1:T(8,128)(2,1)} %bitcast.79) | data formatting | bytes 4194304 | tf_op jit(solution)/shard_map/dot_general | solution.py:46
  48.3 84.4 %all-to-all-done = bf16[16,64,2048]{2,0,1:T(8,128)(2,1)} async-done(((bf16[16,64,2048]{2,0,1:T(8,128)(2,1)}), bf16[16,64,2048]{2,0,1:T(8,128)(2,1)}, u32[]{:S(2)}, u32[]{:S(2)}) %all-to-all-start) | async-done | bytes 4194336 | tf_op jit(solution)/shard_map/all_to_all | solution.py:122
  132.8 4.5 %copy.65 = bf16[16,64,2048]{2,1,0:T(8,128)(2,1)S(1)} copy(bf16[16,64,2048]{2,0,1:T(8,128)(2,1)} %all-to-all-done) | data formatting | bytes 8388608 | tf_op jit(solution)/shard_map/all_to_all | solution.py:122
  137.3 6.5 %multiply_reduce_fusion = (f32[16,64]{1,0:T(8,128)S(1)}, f32[16,64,2048]{2,1,0:T(8,128)}) fusion(s32[]{:T(128)S(6)} %select_n.168, bf16[16,64,2048]{2,1,0:T(8,128)(2,1)S(1)} %copy.65), kind=kLoop, calls=%fused_computation.16 | loop fusion | flops 12581888 | bytes 12587012 | tf_op jit(solution)/shard_map/reduce_sum | solution.py:21
  143.8 4.3 %multiply_convert_fusion = bf16[16,64,2048]{2,1,0:T(8,128)(2,1)S(1)} fusion(f32[16,64,2048]{2,1,0:T(8,128)} %get-tuple-element.17, f32[2048]{0:T(1024)S(1)} %convert_element_type.122, f32[16,64]{1,0:T(8,128)S(1)} %add_rsqrt_fusion.2), kind=kLoop, calls=%fused_computation.15 | loop fusion | flops 6291456 | bytes 12595200 | tf_op jit(solution)/shard_map/convert_element_type | solution.py:130
  149.6 2.7 %fusion.3 = bf16[1024,2048]{1,0:T(8,128)(2,1)} fusion(f32[16,64,2048]{2,1,0:T(8,128)S(1)} %copy-done.1, f32[2048]{0:T(1024)S(1)} %convert_element_type.122, f32[1024]{0:T(1024)S(1)} %rsqrt.29), kind=kLoop, calls=%fused_computation.12 | loop fusion | flops 6291456 | bytes 12595200 | tf_op jit(solution)/shard_map/convert_element_type | solution.py:130
  153.0 2.4 multiply_reduce_fusion.1
  157.1 2.4 copy.70
  160.9 3.9 %multiply_reduce_fusion.2 = (f32[1024,2]{0,1:T(2,128)S(1)}, f32[1024,2,128]{0,2,1:T(8,128)S(1)}) fusion(bf16[1024,2048,1]{1,0,2:T(8,128)(2,1)} %bitcast.76, bf16[2,128,2048]{2,1,0:T(8,128)(2,1)} %bitcast.83), kind=kOutput, calls=%fused_computation.41 | convolution fusion | flops 1074264064 | bytes 6299648 | tf_op jit(solution)/shard_map/dot_general | solution.py:49
  167.0 2.1 convolution_convert_fusion
  169.1 11.5 %fusion.38 = (f32[2,2,1024]{2,1,0:T(2,128)S(1)}, f32[2,2,1024,1024]{2,3,1,0:T(8,128)}) fusion(pred[1024,1024]{0,1:T(8,128)(4,1)S(1)} %copy-done.5, bf16[1024,2,2,64]{3,0,2,1:T(8,128)(2,1)} %copy.70, bf16[1024,2,2,64]{3,0,2,1:T(8,128)(2,1)} %copy.69, bf16[1024,2,64]{0,2,1:T(8,128)(2,1)} %get-tuple-element.21, bf16[1024,2,64]{0,2,1:T(8,128)(2,1)S(1)} %get-tuple-element.20), kind=kOutput, calls=%fused_computation.108 | convolution fusion | flops 1093665792 | bytes 19415040 | tf_op jit(solution)/shard_map/sub | solution.py:76
  180.6 7.2 %fusion.15 = bf16[1024,2,2,128]{0,3,2,1:T(8,128)(2,1)S(1)} fusion(bf16[1024,2,128,1]{0,2,3,1:T(8,128)(2,1)} %bitcast.84, f32[2,2,1024,1024]{2,3,1,0:T(8,128)} %get-tuple-element.31, f32[2,2,1024]{2,1,0:T(2,128)S(1)} %get-tuple-element.30), kind=kOutput, calls=%fused_computation.31 | convolution fusion | flops 1082654720 | bytes 18366464 | tf_op jit(solution)/shard_map/kgqs,skd->qkgd/dot_general | solution.py:78
  187.9 2.0 copy.73
  192.2 1.5 copy.74
  193.7 5.6 %all-to-all-start.1 = ((bf16[16,64,512]{2,0,1:T(8,128)(2,1)}), bf16[16,64,512]{2,0,1:T(8,128)(2,1)}, u32[]{:S(2)}, u32[]{:S(2)}) async-start(bf16[16,64,512]{2,0,1:T(8,128)(2,1)} %copy.74), calls=%async_computation.1 | async-start | bytes 2097152 | tf_op jit(solution)/shard_map/all_to_all | solution.py:136
  200.4 27.7 %all-to-all-done.1 = bf16[16,64,512]{2,0,1:T(8,128)(2,1)} async-done(((bf16[16,64,512]{2,0,1:T(8,128)(2,1)}), bf16[16,64,512]{2,0,1:T(8,128)(2,1)}, u32[]{:S(2)}, u32[]{:S(2)}) %all-to-all-start.1) | async-done | bytes 1048608 | tf_op jit(solution)/shard_map/all_to_all | solution.py:136
  228.1 1.8 copy.75
  232.4 4.5 %all-to-all-start.2 = ((bf16[4,256,512]{1,2,0:T(8,128)(2,1)}), bf16[4,256,512]{1,2,0:T(8,128)(2,1)}, u32[]{:S(2)}, u32[]{:S(2)}) async-start(bf16[4,256,512]{1,2,0:T(8,128)(2,1)} %stack.6), calls=%async_computation.2 | async-start | bytes 2097152 | tf_op jit(solution)/shard_map/all_to_all | solution.py:13
  239.4 11.8 %all-to-all-done.2 = bf16[4,256,512]{1,2,0:T(8,128)(2,1)} async-done(((bf16[4,256,512]{1,2,0:T(8,128)(2,1)}), bf16[4,256,512]{1,2,0:T(8,128)(2,1)}, u32[]{:S(2)}, u32[]{:S(2)}) %all-to-all-start.2) | async-done | bytes 1048608 | tf_op jit(solution)/shard_map/all_to_all | solution.py:13
  251.2 1.9 convolution_convert_fusion.1
  253.1 1.7 add_convert_fusion.1
  (80 shorter events, 25.4 us)
Async XLA Ops:
  0.6 250.5 %copy-start = (bf16[2048,512]{1,0:T(8,128)(2,1)S(1)}, bf16[2048,512]{1,0:T(8,128)(2,1)}, u32[]{:S(2)}) copy-start(bf16[2048,512]{1,0:T(8,128)(2,1)} %param.19) | copy-start | bytes 6291460
  24.3 15.6 %copy-start.10 = (bf16[2048]{0:T(1024)(128)(2,1)S(1)}, bf16[2048]{0:T(1024)(128)(2,1)}, u32[]{:S(2)}) copy-start(bf16[2048]{0:T(1024)(128)(2,1)} %param.13) | copy-start | bytes 12292
  24.3 108.4 %all-to-all-start = ((bf16[16,64,2048]{2,0,1:T(8,128)(2,1)}), bf16[16,64,2048]{2,0,1:T(8,128)(2,1)}, u32[]{:S(2)}, u32[]{:S(2)}) async-start(bf16[16,64,2048]{2,0,1:T(8,128)(2,1)} %fusion.10), calls=%async_computation | async-start | bytes 8388608 | tf_op jit(solution)/shard_map/all_to_all | solution.py:122
  36.7 7.2 %copy-start.12 = (bf16[128]{0:T(256)(128)(2,1)S(1)}, bf16[128]{0:T(256)(128)(2,1)}, u32[]{:S(2)}) copy-start(bf16[128]{0:T(256)(128)(2,1)} %param.17) | copy-start | bytes 772
  36.7 7.2 %copy-start.6 = (bf16[2048,256]{1,0:T(8,128)(2,1)S(1)}, bf16[2048,256]{1,0:T(8,128)(2,1)}, u32[]{:S(2)}) copy-start(bf16[2048,256]{1,0:T(8,128)(2,1)} %param.15) | copy-start | bytes 3145732
  36.7 8.6 %copy-start.13 = (bf16[128]{0:T(256)(128)(2,1)S(1)}, bf16[128]{0:T(256)(128)(2,1)}, u32[]{:S(2)}) copy-start(bf16[128]{0:T(256)(128)(2,1)} %param.18) | copy-start | bytes 772
  143.8 5.8 %copy-start.1 = (f32[16,64,2048]{2,1,0:T(8,128)S(1)}, f32[16,64,2048]{2,1,0:T(8,128)}, u32[]{:S(2)}) copy-start(f32[16,64,2048]{2,1,0:T(8,128)} %get-tuple-element.17) | copy-start | bytes 25165828
  149.6 3.4 %copy-start.3 = (bf16[16,64,2048]{2,1,0:T(8,128)(2,1)}, bf16[16,64,2048]{2,1,0:T(8,128)(2,1)S(1)}, u32[]{:S(2)}) copy-start(bf16[16,64,2048]{2,1,0:T(8,128)(2,1)S(1)} %multiply_convert_fusion) | copy-start | bytes 12582916
  149.6 3.4 %copy-start.4 = (bf16[512,2048]{1,0:T(8,128)(2,1)S(1)}, bf16[512,2048]{1,0:T(8,128)(2,1)}, u32[]{:S(2)}) copy-start(bf16[512,2048]{1,0:T(8,128)(2,1)} %copy.84) | copy-start | bytes 6291460
  160.9 5.0 %copy-start.11 = (bf16[2048,256]{1,0:T(8,128)(2,1)S(1)}, bf16[2048,256]{1,0:T(8,128)(2,1)}, u32[]{:S(2)}) copy-start(bf16[2048,256]{1,0:T(8,128)(2,1)} %param.16) | copy-start | bytes 3145732
  164.8 2.3 copy-start.2
  167.0 2.1 copy-start.7
  167.0 2.1 copy-start.5
  193.7 34.4 %all-to-all-start.1 = ((bf16[16,64,512]{2,0,1:T(8,128)(2,1)}), bf16[16,64,512]{2,0,1:T(8,128)(2,1)}, u32[]{:S(2)}, u32[]{:S(2)}) async-start(bf16[16,64,512]{2,0,1:T(8,128)(2,1)} %copy.74), calls=%async_computation.1 | async-start | bytes 2097152 | tf_op jit(solution)/shard_map/all_to_all | solution.py:136
  231.1 5.8 %copy-start.8 = (bf16[1024,2,64]{0,2,1:T(8,128)(2,1)S(1)}, bf16[1024,2,64]{0,2,1:T(8,128)(2,1)}, u32[]{:S(2)}) copy-start(bf16[1024,2,64]{0,2,1:T(8,128)(2,1)} %copy-done.7) | copy-start | bytes 786436
  231.1 5.8 %copy-start.9 = (bf16[1024,2,64]{0,2,1:T(8,128)(2,1)S(1)}, bf16[1024,2,64]{0,2,1:T(8,128)(2,1)}, u32[]{:S(2)}) copy-start(bf16[1024,2,64]{0,2,1:T(8,128)(2,1)} %get-tuple-element.21) | copy-start | bytes 786436
  232.4 18.7 %all-to-all-start.2 = ((bf16[4,256,512]{1,2,0:T(8,128)(2,1)}), bf16[4,256,512]{1,2,0:T(8,128)(2,1)}, u32[]{:S(2)}, u32[]{:S(2)}) async-start(bf16[4,256,512]{1,2,0:T(8,128)(2,1)} %stack.6), calls=%async_computation.2 | async-start | bytes 2097152 | tf_op jit(solution)/shard_map/all_to_all | solution.py:13
